TPU v7x, 512 devices: a whole 4x4x16 slice. The times are simulated.
512 devices in a mesh: dp: 4 (over x), ctx: 16 (over z), mp: 8 (over y, core).
Axes of the slice: x: 4, y: 4, z: 16, core: 2. Of those that a mesh axis runs over, the one named last changes fastest.
Arguments:
- tokens: bfloat16 [4, 2048, 4096], P('dp', 'ctx'), may hold values from -52 to 52
- x_weight: bfloat16 [4096, 8192], P(('dp', 'ctx'), 'mp'), may hold values from -0.09375 to 0.09375
- bc_weight: bfloat16 [4096, 1024], P(('dp', 'ctx'), 'mp'), may hold values from -0.09375 to 0.09375
- dt_weight: bfloat16 [4096, 128], P(('dp', 'ctx'), 'mp'), may hold values from -0.0234375 to 0.0234375
- conv_x: float32 [5, 8192], P(None, 'mp'), may hold values from -0.5 to 0.5
- conv_bc: float32 [5, 1024], P(None, 'mp'), may hold values from -0.5 to 0.5
- dt_bias: float32 [128], P('mp'), may hold values from -4.5 to -2.5
- a_log: float32 [128], P('mp')
- d_skip: float32 [128], P('mp'), may hold values from 0.5 to 1.5
- norm_gain: float32 [8192], P('mp'), may hold values from 0.5 to 1.5
Outputs:
- mixer_out: bfloat16 [4, 2048, 8192], P('dp', 'ctx', 'mp')
- kurtosis: float32 [4096], P('mp')
All inputs are finite; a program needn't handle non-finite values.
Results may differ from a plain program's by a relative error of at most 0.015.
Values may be sent and summed in bfloat16 or wider, within the bound.
No kernel may reach another device: no remote copies, remote signals or barrier semaphores. Data moves between devices by JAX's collectives and lax.ppermute only.
A program may use at most 64 MiB of HBM per device.

v0:
```python
import jax
import jax.numpy as jnp
from jax import lax
from jax.sharding import PartitionSpec as P

ROOT = 64
HEADS = 128
G = 4
NS = 128
HIGH = lax.Precision.HIGHEST


def passed_along(value, axis, steps):
    count = lax.axis_size(axis)
    first, last = (max(0, -steps), min(count, count - steps))
    return lax.ppermute(value, axis, [(source, source + steps) for source in range(first, last)])


def entering(decay, contrib, axis):
    length, place = (lax.axis_size(axis), lax.axis_index(axis))
    lanes = contrib.shape[-1]
    rows = contrib.size // lanes
    tail = jnp.zeros((8, lanes), jnp.float32).at[0, : decay.size].set(decay.reshape(-1))
    flat = jnp.concatenate([contrib.reshape(rows, lanes), tail]).astype(jnp.bfloat16)
    everything = lax.all_gather(flat, axis).astype(jnp.float32)
    states = everything[:, :rows].reshape((length,) + contrib.shape)
    decays = everything[:, rows, : decay.size].reshape((length,) + decay.shape)
    source = lax.broadcasted_iota(jnp.int32, (length, length), 0)
    between = lax.broadcasted_iota(jnp.int32, (length, length), 1)
    inside = jnp.logical_and(between > source, between < place)
    factors = jnp.where(inside[:, :, None, None], decays[None], 1.0)
    weights = jnp.prod(factors, 1)
    weights = jnp.where((source[:, 0] < place)[:, None, None], weights, 0.0)
    return jnp.einsum("jgh,jghpn->ghpn", weights, states, precision=HIGH)


def hadamard_signs(sign_order):
    row_index = lax.broadcasted_iota(jnp.int32, (sign_order, sign_order), 0)
    col_index = lax.broadcasted_iota(jnp.int32, (sign_order, sign_order), 1)
    common = jnp.bitwise_and(row_index, col_index)
    parity = jnp.zeros((sign_order, sign_order), jnp.int32)
    for bit_index in range(sign_order.bit_length() - 1):
        parity = parity + jnp.bitwise_and(jnp.right_shift(common, bit_index), 1)
    return 1.0 - 2.0 * jnp.bitwise_and(parity, 1).astype(jnp.float32)


def kurtosis_from(powers, row_count):
    average = powers[0] / row_count
    second = powers[1] / row_count - average * average
    fourth = (
        powers[3] / row_count
        - 4.0 * average * powers[2] / row_count
        + 6.0 * average * average * powers[1] / row_count
        - 3.0 * average * average * average * average
    )
    return fourth / (second * second + 1e-06)


def shards(
    tokens, x_weight, bc_weight, dt_weight, conv_x, conv_bc, dt_bias, a_log, d_skip, norm_gain
):
    tok_rows = tokens.shape[1]
    model_width = tokens.shape[2]
    signs = hadamard_signs(ROOT)
    blocks = tokens.reshape(tok_rows, ROOT, ROOT)
    first_pass = jnp.einsum(
        "tab,ac->tcb", blocks, signs.astype(jnp.bfloat16), preferred_element_type=jnp.float32
    )
    second = jnp.einsum("tcb,bd->tcd", first_pass, signs, precision=HIGH)
    rotated = (second.reshape(tok_rows, model_width) / ROOT).astype(jnp.bfloat16)
    channel_share = model_width // lax.axis_size("mp")
    own_cols = lax.dynamic_slice_in_dim(
        rotated, lax.axis_index("mp") * channel_share, channel_share, 1
    ).astype(jnp.float32)
    square = own_cols * own_cols
    powers = jnp.stack(
        [
            jnp.sum(own_cols, 0),
            jnp.sum(square, 0),
            jnp.sum(square * own_cols, 0),
            jnp.sum(square * square, 0),
        ]
    )
    row_count = float(tok_rows * lax.axis_size("dp") * lax.axis_size("ctx"))
    totals = lax.psum(lax.psum(powers, "ctx"), "dp")
    totals, rotated = lax.optimization_barrier((totals, rotated))
    kurtosis = kurtosis_from(totals, row_count)
    local_panel = jnp.concatenate([x_weight, bc_weight, dt_weight], 1)
    panel = lax.all_gather(local_panel, ("dp", "ctx"), axis=0, tiled=True)
    both = jnp.dot(rotated, panel, preferred_element_type=jnp.float32)
    x_end = x_weight.shape[1]
    bc_end = x_end + bc_weight.shape[1]
    projected = (both[:, :x_end], both[:, x_end:bc_end], both[:, bc_end:])
    x_cols = x_weight.shape[1]
    joined = jnp.concatenate(
        [projected[0].astype(jnp.bfloat16), projected[1].astype(jnp.bfloat16)], 1
    )
    dt_proj = lax.optimization_barrier(projected[2].astype(jnp.bfloat16))
    conv_taps = jnp.concatenate([conv_x, conv_bc], 1)
    kernel = conv_taps.shape[0] - 1
    rim_rows = passed_along(joined[tok_rows - (kernel - 1) :], "ctx", 1)
    padded = jnp.concatenate([rim_rows, joined], 0)
    conv_sum = conv_taps[kernel]
    for tap_index in range(kernel):
        conv_sum = conv_sum + conv_taps[tap_index] * padded[tap_index : tap_index + tok_rows]
    convolved = jax.nn.silu(conv_sum).astype(jnp.bfloat16)
    x_conv = convolved[:, :x_cols]
    group_all = lax.all_gather(convolved[:, x_cols:], "mp", axis=1, tiled=True)
    heads_dev = dt_weight.shape[1]
    head_size = x_cols // heads_dev
    per_group = HEADS // G
    groups_here = max(1, heads_dev // per_group)
    heads_local = heads_dev // groups_here
    first_group = lax.axis_index("mp") * heads_dev // per_group
    write_all = group_all[:, : G * NS].reshape(tok_rows, G, NS)
    read_all = group_all[:, G * NS :].reshape(tok_rows, G, NS)
    write_here = lax.dynamic_slice_in_dim(write_all, first_group, groups_here, 1)
    read_here = lax.dynamic_slice_in_dim(read_all, first_group, groups_here, 1)
    step_size = jax.nn.softplus(dt_proj.astype(jnp.float32) + dt_bias)
    decay_rate = step_size * jnp.exp(a_log)
    cumulative = jnp.cumsum(decay_rate, 0)
    block_end = cumulative[-1]
    causal = lax.broadcasted_iota(jnp.int32, (tok_rows, tok_rows), 0) >= lax.broadcasted_iota(
        jnp.int32, (tok_rows, tok_rows), 1
    )
    spread = cumulative.T[:, :, None] - cumulative.T[:, None, :]
    decay_mask = jnp.where(causal, jnp.exp(-jnp.where(causal, spread, 0.0)), 0.0)
    scores = jnp.einsum("tgn,sgn->gts", read_here, write_here, preferred_element_type=jnp.float32)
    weights = (
        scores[:, None]
        * decay_mask.reshape(groups_here, heads_local, tok_rows, tok_rows)
        * step_size.T.reshape(groups_here, heads_local, 1, tok_rows)
    ).astype(jnp.bfloat16)
    x_heads = x_conv.reshape(tok_rows, groups_here, heads_local, head_size)
    within_block = jnp.einsum(
        "ghts,sghp->tghp", weights, x_heads, preferred_element_type=jnp.float32
    )
    update = (
        (jnp.exp(-(block_end - cumulative)) * step_size).reshape(
            tok_rows, groups_here, heads_local
        )[..., None]
        * x_heads
    ).astype(jnp.bfloat16)
    contrib = jnp.einsum("sghp,sgn->ghpn", update, write_here, preferred_element_type=jnp.float32)
    carried = entering(jnp.exp(-block_end).reshape(groups_here, heads_local), contrib, "ctx")
    from_before = jnp.exp(-cumulative).reshape(tok_rows, groups_here, heads_local)[
        ..., None
    ] * jnp.einsum("tgn,ghpn->tghp", read_here.astype(jnp.float32), carried, precision=HIGH)
    output_raw = (
        within_block
        + from_before
        + d_skip.reshape(groups_here, heads_local)[None, :, :, None] * x_heads.astype(jnp.float32)
    )
    mean_square = jnp.mean(output_raw * output_raw, -1, keepdims=True)
    normed = (
        output_raw
        * lax.rsqrt(mean_square + 1e-05)
        * norm_gain.reshape(groups_here, heads_local, head_size)
    )
    return (normed.reshape(1, tok_rows, x_cols).astype(jnp.bfloat16), kurtosis)


def solution(mesh):
    return jax.shard_map(
        shards,
        mesh=mesh,
        in_specs=(
            P("dp", "ctx", None),
            P(("dp", "ctx"), "mp"),
            P(("dp", "ctx"), "mp"),
            P(("dp", "ctx"), "mp"),
            P(None, "mp"),
            P(None, "mp"),
            P("mp"),
            P("mp"),
            P("mp"),
            P("mp"),
        ),
        out_specs=(P("dp", "ctx", "mp"), P("mp")),
        check_vma=False,
    )
```

profile of v0, /device:TPU:4, one launch (start us, length us, event | category | flops | bytes accessed | tf_op | source)
XLA Modules:
  0.0 302.1 jit_solution(1857820000837005802)
XLA Ops:
  7.2 0.0 all-gather.3.cloned.1.call-start
  7.2 0.8 copy.43
  8.0 1.6 pad_maximum_fusion.1
  9.6 0.0 all-gather.3.cloned.1.call-update
  9.6 0.0 all-gather.5.cloned.1.call-start
  9.7 0.0 copy-start.5
  9.7 0.0 copy-start.1
  9.7 0.0 copy-start.3
  9.7 1.6 copy.40
  11.3 0.9 convolution_bitcast_fusion
  12.2 3.3 %multiply_convert_fusion = bf16[128,64,64]{0,2,1:T(8,128)(2,1)S(1)} fusion(f32[128,64,64]{0,1,2:T(8,128)S(1)} %convolution_bitcast_fusion), kind=kOutput, calls=%fused_computation.5 | convolution fusion | flops 403791872 | bytes 3145728 | tf_op jit(solution)/shard_map/tcb,bd->tcd/dot_general | solution.py:69
  15.6 0.3 convert_reduce_fusion
  15.9 37.2 %psum.14 = f32[4,512]{1,0:T(4,128)S(1)} all-reduce(f32[4,512]{1,0:T(4,128)S(1)} %pad_maximum_fusion.2), channel_id=1, replica_groups=mesh['dp'=4,'ctx'=16,'mp'=8] {'ctx'}, use_global_device_ids=true, to_apply=%region_4.0 | all-reduce | flops 2048 | bytes 16384 | tf_op jit(solution)/shard_map/psum | solution.py:85
  53.1 8.4 %psum.15 = f32[4,512]{1,0:T(4,128)S(1)} all-reduce(f32[4,512]{1,0:T(4,128)S(1)} %psum.14), channel_id=1, replica_groups=mesh['dp'=4,'ctx'=16,'mp'=8] {'dp'}, use_global_device_ids=true, to_apply=%region_5.0 | all-reduce | flops 2048 | bytes 16384 | tf_op jit(solution)/shard_map/psum | solution.py:85
  61.6 0.1 slice_reduce_fusion.4
  61.7 0.0 copy-start.4
  61.7 116.0 %all-gather.3.cloned.1.call-done = bf16[4096,1168]{1,0:T(8,128)(2,1)} async-done(((bf16[64,1168]{1,0:T(8,128)(2,1)}), bf16[4096,1168]{1,0:T(8,128)(2,1)}) %all-gather.3.cloned.1.call-update) | async-done | bytes 9568272 | tf_op jit(solution)/shard_map/all_gather | solution.py:89
  177.7 8.0 %convolution_convert_fusion = bf16[128,1168]{0,1:T(8,128)(2,1)S(1)} fusion(bf16[128,4096]{0,1:T(8,128)(2,1)S(1)} %bitcast.81, bf16[4096,1168]{1,0:T(8,128)(2,1)} %all-gather.3.cloned.1.call-done), kind=kOutput, calls=%fused_computation.2 | convolution fusion | flops 1224886272 | bytes 10915840 | tf_op jit(solution)/shard_map/dot_general | solution.py:90
  185.7 0.1 slice.121
  185.9 0.1 broadcast_multiply_fusion
  186.0 0.1 copy.45
  186.1 0.2 reduce_window_sum.11
  186.2 0.1 copy.49
  186.3 3.3 %collective-permute-start = (bf16[3,1152]{0,1:T(8,128)(2,1)S(1)}, bf16[3,1152]{0,1:T(8,128)(2,1)S(1)}, u32[]{:S(2)}, u32[]{:S(2)}) collective-permute-start(bf16[3,1152]{0,1:T(8,128)(2,1)S(1)} %slice.121), channel_id=1, source_target_pairs={{0,8},{8,16},{16,24},{24,32},{32,40},{40,48},{48,56},{56,64},{64,7... | collective-permute-start | bytes 20744 | tf_op jit(solution)/shard_map/ppermute | solution.py:16
  189.6 0.1 fusion.60
  189.7 4.1 %collective-permute-done = bf16[3,1152]{0,1:T(8,128)(2,1)S(1)} collective-permute-done((bf16[3,1152]{0,1:T(8,128)(2,1)S(1)}, bf16[3,1152]{0,1:T(8,128)(2,1)S(1)}, u32[]{:S(2)}, u32[]{:S(2)}) %collective-permute-start) | collective-permute-done | bytes 6944 | tf_op jit(solution)/shard_map/ppermute | solution.py:16
  193.8 1.4 multiply_convert_fusion.2
  195.2 13.4 %all_gather.11 = bf16[128,1024]{0,1:T(8,128)(2,1)S(1)} all-gather(bf16[128,128]{0,1:T(8,128)(2,1)S(1)} %slice.131), channel_id=1, replica_groups=mesh['dp'=4,'ctx'=16,'mp'=8] {'mp'}, dimensions={1}, use_global_device_ids=true | all-gather | bytes 294912 | tf_op jit(solution)/shard_map/all_gather | solution.py:108
  208.6 0.1 multiply_convert_fusion.5
  208.7 0.2 fusion.9
  208.9 0.7 fusion.22
  209.7 0.0 all-gather.5.cloned.1.call-update
  209.7 0.1 mul.242
  209.8 0.6 fusion.39
  210.5 0.1 copy.48
  210.5 0.1 copy.46
  210.6 0.2 fusion.26
  210.8 75.6 %all-gather.5.cloned.1.call-done = bf16[16,1032,128]{2,1,0:T(8,128)(2,1)} async-done(((bf16[1,1032,128]{2,1,0:T(8,128)(2,1)}), bf16[16,1032,128]{2,1,0:T(8,128)(2,1)}) %all-gather.5.cloned.1.call-update) | async-done | bytes 4227088 | tf_op jit(solution)/shard_map/all_gather | solution.py:25
  286.3 0.8 slice_convert_fusion
  287.1 0.1 select_reduce_fusion
  287.2 0.1 select_bitcast_fusion
  287.3 0.1 copy.51
  287.4 2.2 slice-done
  289.6 3.6 %fusion = f32[16,1,64,128]{3,1,2,0:T(1,128)S(1)} fusion(f32[16,16,1,1]{0,2,3,1:T(1,128)S(1)} %copy.51, bf16[16,16,64,128]{3,2,1,0:T(8,128)(2,1)S(1)} %bitcast.79), kind=kOutput, calls=%fused_computation | convolution fusion | flops 25165824 | bytes 4719616 | tf_op jit(solution)/shard_map/jgh,jghpn->ghpn/dot_general | solution.py:34
  293.1 0.4 fusion.8
  293.5 0.6 multiply_reduce_fusion
  294.2 0.2 multiply_convert_fusion.4
  294.4 0.9 copy.50
  (29 shorter events, 0.2 us)
Async XLA Ops:
  7.2 170.5 %all-gather.3.cloned.1.call-start = ((), (), s32[]{:S(2)}) async-start(), calls=%async_computation | async-start | bytes 10649600 | tf_op jit(solution)/shard_map/all_gather | solution.py:89
  9.6 276.7 %all-gather.5.cloned.1.call-start = ((), (), s32[]{:S(2)}) async-start(), calls=%async_computation.1 | async-start | bytes 4491264 | tf_op jit(solution)/shard_map/all_gather | solution.py:25
  9.7 51.8 %copy-start.5 = (f32[16]{0:T(128)S(1)}, f32[16]{0:T(128)}, u32[]{:S(2)}) copy-start(f32[16]{0:T(128)} %param.19) | copy-start | bytes 196
  9.7 51.9 %copy-start.1 = (f32[5,1024]{1,0:T(8,128)S(1)}, f32[5,1024]{1,0:T(8,128)}, u32[]{:S(2)}) copy-start(f32[5,1024]{1,0:T(8,128)} %param.16) | copy-start | bytes 61444
  9.7 51.9 %copy-start.3 = (f32[5,128]{1,0:T(8,128)S(1)}, f32[5,128]{1,0:T(8,128)}, u32[]{:S(2)}) copy-start(f32[5,128]{1,0:T(8,128)} %param.17) | copy-start | bytes 7684
  61.7 124.2 %copy-start.4 = (f32[16]{0:T(128)S(1)}, f32[16]{0:T(128)}, u32[]{:S(2)}) copy-start(f32[16]{0:T(128)} %param.18) | copy-start | bytes 196
  185.7 24.0 %copy-start.2 = (f32[1024]{0:T(1024)S(1)}, f32[1024]{0:T(1024)}, u32[]{:S(2)}) copy-start(f32[1024]{0:T(1024)} %param.21) | copy-start | bytes 12292
  186.3 7.5 %collective-permute-start = (bf16[3,1152]{0,1:T(8,128)(2,1)S(1)}, bf16[3,1152]{0,1:T(8,128)(2,1)S(1)}, u32[]{:S(2)}, u32[]{:S(2)}) collective-permute-start(bf16[3,1152]{0,1:T(8,128)(2,1)S(1)} %slice.121), channel_id=1, source_target_pairs={{0,8},{8,16},{16,24},{24,32},{32,40},{40,48},{48,56},{56,64},{64,7... | collective-permute-start | bytes 20744 | tf_op jit(solution)/shard_map/ppermute | solution.py:16
  195.2 92.2 %copy-start = (bf16[128,1152]{0,1:T(8,128)(2,1)}, bf16[128,1152]{0,1:T(8,128)(2,1)S(1)}, u32[]{:S(2)}) copy-start(bf16[128,1152]{0,1:T(8,128)(2,1)S(1)} %multiply_convert_fusion.2) | copy-start | bytes 884740
  287.4 2.2 slice-start
  287.4 6.1 %copy-start.6 = (f32[16]{0:T(128)S(1)}, f32[16]{0:T(128)}, u32[]{:S(2)}) copy-start(f32[16]{0:T(128)} %param.20) | copy-start | bytes 196
  289.6 4.0 %slice-start.1 = ((bf16[128,1152]{0,1:T(8,128)(2,1)}), bf16[128,1024]{0,1:T(8,128)(2,1)S(1)}, s32[]{:S(2)}) async-start(bf16[128,1152]{0,1:T(8,128)(2,1)} %copy-done), calls=%async_computation.3 | async-start | bytes 524288 | tf_op jit(solution)/shard_map/slice | solution.py:107
Sparse Core Ops, SparseCore 0:
  11.5 166.0 all-gather.2
  209.8 76.4 all-gather.4
where the time goes:
time: 302 us
  waiting for transfers between devices  196 us (65%)
  blocking collectives  58.9 us (20%)
  matrix products  17.2 us (6%)
  between operations  14.4 us (5%)
  other arithmetic  6.37 us (2%)
  local copies, waits for them, and re-layouts  6.17 us (2%)
  starting transfers between devices  3.33 us (1%)
    all_gather x1, waiting for transfers between devices, shards(): panel = lax.all_gather(local_panel, ('dp', 'ctx'), axis=0, tiled=True)  116 us
    all_gather x1, waiting for transfers between devices, entering(): everything = lax.all_gather(flat, axis).astype(jnp.float32)  75.6 us
    psum x2, blocking collectives, shards(): totals = lax.psum(lax.psum(powers, 'ctx'), 'dp')  45.6 us
    all_gather x1, blocking collectives, shards(): group_all = lax.all_gather(convolved[:, x_cols:], 'mp', axis=1, tiled=True)  13.4 us
    dot_general x1, matrix products, shards(): both = jnp.dot(rotated, panel, preferred_element_type=jnp.float32)  8.01 us
  transfers between devices with their start and end apart: 3, of which 3 were waited for; matrix products, arithmetic and copies ran while one was open for 2% of the time, Pallas kernels for 0%

commit v1 on v0

--- a/solution.py
+++ b/solution.py
@@ -86,7 +86,12 @@
     totals, rotated = lax.optimization_barrier((totals, rotated))
     kurtosis = kurtosis_from(totals, row_count)
     local_panel = jnp.concatenate([x_weight, bc_weight, dt_weight], 1)
-    panel = lax.all_gather(local_panel, ("dp", "ctx"), axis=0, tiled=True)
+    panel = jnp.concatenate(
+        lax.all_to_all(
+            jnp.stack([local_panel] * lax.axis_size(("dp", "ctx"))), ("dp", "ctx"), 0, 0
+        ),
+        axis=0,
+    )
     both = jnp.dot(rotated, panel, preferred_element_type=jnp.float32)
     x_end = x_weight.shape[1]
     bc_end = x_end + bc_weight.shape[1]

time: 302 us -> 644 us (2.13)
  the two profiles are of different devices: /device:TPU:4 before, /device:TPU:2 now
where the time goes in v1:
time: 644 us
  blocking collectives  492 us (76%)
  waiting for transfers between devices  83.2 us (13%)
  starting transfers between devices  20.7 us (3%)
  matrix products  17.2 us (3%)
  between operations  14.4 us (2%)
  local copies, waits for them, and re-layouts  10.3 us (2%)
    psum x2, blocking collectives, shards(): totals = lax.psum(lax.psum(powers, 'ctx'), 'dp')  479 us
    all_gather x1, waiting for transfers between devices, entering(): everything = lax.all_gather(flat, axis).astype(jnp.float32)  79.2 us
    all_to_all x1, starting transfers between devices, shards(): lax.all_to_all(jnp.stack([local_panel] * lax.axis_size(('dp', 'ctx'))), (...  18.9 us
    all_gather x1, blocking collectives, shards(): group_all = lax.all_gather(convolved[:, x_cols:], 'mp', axis=1, tiled=True)  13.4 us
  transfers between devices with their start and end apart: 3, of which 2 were waited for; matrix products, arithmetic and copies ran while one was open for 1% of the time, Pallas kernels for 0%

profile of v1, /device:TPU:2, one launch (start us, length us, event | category | flops | bytes accessed | tf_op | source)
XLA Modules:
  0.0 643.8 jit_solution(1447151864061325425)
XLA Ops:
  7.2 0.8 copy.43
  7.9 0.9 pad_maximum_fusion.1
  8.9 5.1 stack.17
  14.0 18.9 %all-to-all-start = ((bf16[64,64,1168]{2,1,0:T(8,128)(2,1)}), bf16[64,64,1168]{2,1,0:T(8,128)(2,1)}, u32[]{:S(2)}, u32[]{:S(2)}) async-start(bf16[64,64,1168]{2,1,0:T(8,128)(2,1)} %stack.17), calls=%async_computation | async-start | bytes 20971520 | tf_op jit(solution)/shard_map/all_to_all | solution.py:90
  32.9 0.0 all-gather.2.cloned.1.call-start
  33.0 0.0 copy-start.6
  33.0 0.0 copy-start.2
  33.0 0.0 copy-start.4
  33.1 0.7 copy.40
  33.7 0.9 convolution_bitcast_fusion
  34.6 3.3 multiply_convert_fusion
  37.9 0.3 convert_reduce_fusion
  38.3 469.9 %psum.14 = f32[4,512]{1,0:T(4,128)S(1)} all-reduce(f32[4,512]{1,0:T(4,128)S(1)} %pad_maximum_fusion.2), channel_id=1, replica_groups=mesh['dp'=4,'ctx'=16,'mp'=8] {'ctx'}, use_global_device_ids=true, to_apply=%region_4.0 | all-reduce | flops 2048 | bytes 16384 | tf_op jit(solution)/shard_map/psum | solution.py:85
  508.2 9.0 %psum.15 = f32[4,512]{1,0:T(4,128)S(1)} all-reduce(f32[4,512]{1,0:T(4,128)S(1)} %psum.14), channel_id=1, replica_groups=mesh['dp'=4,'ctx'=16,'mp'=8] {'dp'}, use_global_device_ids=true, to_apply=%region_5.0 | all-reduce | flops 2048 | bytes 16384 | tf_op jit(solution)/shard_map/psum | solution.py:85
  517.3 0.1 slice_reduce_fusion.4
  517.4 0.0 copy-start.5
  517.4 8.0 %convolution_convert_fusion = bf16[128,1168]{0,1:T(8,128)(2,1)S(1)} fusion(bf16[128,4096]{0,1:T(8,128)(2,1)S(1)} %bitcast.82, bf16[4096,1168]{1,0:T(8,128)(2,1)} %bitcast.9), kind=kOutput, calls=%fused_computation.2 | convolution fusion | flops 1224886272 | bytes 10915840 | tf_op jit(solution)/shard_map/dot_general | solution.py:95
  525.4 0.0 copy-start.3
  525.5 0.1 slice.121
  525.6 0.1 broadcast_multiply_fusion
  525.7 0.1 copy.45
  525.8 0.2 reduce_window_sum.11
  526.0 0.1 copy.49
  526.1 1.7 collective-permute-start
  527.8 0.1 fusion.60
  527.9 3.9 collective-permute-done
  531.8 1.4 multiply_convert_fusion.2
  533.3 13.4 %all_gather.7 = bf16[128,1024]{0,1:T(8,128)(2,1)S(1)} all-gather(bf16[128,128]{0,1:T(8,128)(2,1)S(1)} %slice.131), channel_id=1, replica_groups=mesh['dp'=4,'ctx'=16,'mp'=8] {'mp'}, dimensions={1}, use_global_device_ids=true | all-gather | bytes 294912 | tf_op jit(solution)/shard_map/all_gather | solution.py:113
  546.7 0.1 multiply_convert_fusion.5
  546.7 0.2 fusion.9
  547.0 0.7 fusion.22
  547.7 0.0 all-gather.2.cloned.1.call-update
  547.7 0.1 mul.242
  547.9 0.6 fusion.39
  548.5 0.1 copy.48
  548.6 0.1 copy.46
  548.6 0.2 fusion.26
  548.8 79.2 %all-gather.2.cloned.1.call-done = bf16[16,1032,128]{2,1,0:T(8,128)(2,1)} async-done(((bf16[1,1032,128]{2,1,0:T(8,128)(2,1)}), bf16[16,1032,128]{2,1,0:T(8,128)(2,1)}) %all-gather.2.cloned.1.call-update) | async-done | bytes 4227088 | tf_op jit(solution)/shard_map/all_gather | solution.py:25
  628.1 0.8 slice_convert_fusion
  628.8 0.1 select_reduce_fusion
  629.0 0.1 select_bitcast_fusion
  629.0 0.1 copy.51
  629.1 2.2 slice-done
  631.3 3.6 fusion
  634.9 0.4 fusion.8
  635.3 0.6 multiply_reduce_fusion
  635.9 0.2 multiply_convert_fusion.4
  636.1 0.9 copy.50
  (31 shorter events, 0.2 us)
Async XLA Ops:
  14.0 19.0 %copy-start.1 = (bf16[1,128,4096]{2,1,0:T(8,128)(2,1)S(1)}, bf16[1,128,4096]{2,1,0:T(8,128)(2,1)}, u32[]{:S(2)}) copy-start(bf16[1,128,4096]{2,1,0:T(8,128)(2,1)} %param.12) | copy-start | bytes 3145732
  14.0 503.4 %all-to-all-start = ((bf16[64,64,1168]{2,1,0:T(8,128)(2,1)}), bf16[64,64,1168]{2,1,0:T(8,128)(2,1)}, u32[]{:S(2)}, u32[]{:S(2)}) async-start(bf16[64,64,1168]{2,1,0:T(8,128)(2,1)} %stack.17), calls=%async_computation | async-start | bytes 20971520 | tf_op jit(solution)/shard_map/all_to_all | solution.py:90
  32.9 595.1 %all-gather.2.cloned.1.call-start = ((), (), s32[]{:S(2)}) async-start(), calls=%async_computation.1 | async-start | bytes 4491264 | tf_op jit(solution)/shard_map/all_gather | solution.py:25
  33.0 484.2 %copy-start.6 = (f32[16]{0:T(128)S(1)}, f32[16]{0:T(128)}, u32[]{:S(2)}) copy-start(f32[16]{0:T(128)} %param.19) | copy-start | bytes 196
  33.0 484.3 %copy-start.2 = (f32[5,1024]{1,0:T(8,128)S(1)}, f32[5,1024]{1,0:T(8,128)}, u32[]{:S(2)}) copy-start(f32[5,1024]{1,0:T(8,128)} %param.16) | copy-start | bytes 61444
  33.0 484.3 %copy-start.4 = (f32[5,128]{1,0:T(8,128)S(1)}, f32[5,128]{1,0:T(8,128)}, u32[]{:S(2)}) copy-start(f32[5,128]{1,0:T(8,128)} %param.17) | copy-start | bytes 7684
  517.4 8.2 %copy-start.5 = (f32[16]{0:T(128)S(1)}, f32[16]{0:T(128)}, u32[]{:S(2)}) copy-start(f32[16]{0:T(128)} %param.18) | copy-start | bytes 196
  525.4 22.3 %copy-start.3 = (f32[1024]{0:T(1024)S(1)}, f32[1024]{0:T(1024)}, u32[]{:S(2)}) copy-start(f32[1024]{0:T(1024)} %param.21) | copy-start | bytes 12292
  526.1 5.8 collective-permute-start
  533.3 95.8 %copy-start = (bf16[128,1152]{0,1:T(8,128)(2,1)}, bf16[128,1152]{0,1:T(8,128)(2,1)S(1)}, u32[]{:S(2)}) copy-start(bf16[128,1152]{0,1:T(8,128)(2,1)S(1)} %multiply_convert_fusion.2) | copy-start | bytes 884740
  629.1 2.2 slice-start
  629.1 6.1 copy-start.7
  631.3 3.9 slice-start.1
Sparse Core Ops, SparseCore 0:
  547.9 80.1 all-gather.1
